TPU v7x, 128 devices: a whole 4x4x4 slice. The times are simulated.
128 devices in a mesh: pipe: 8 (over z, core), ctx: 16 (over y, x).
Axes of the slice: x: 4, y: 4, z: 4, core: 2. Of those that a mesh axis runs over, the one named last changes fastest.
Arguments:
- grad_in: bfloat16 [8, 4096, 8192], P('pipe', 'ctx'), may hold values from -6 to 6
- query: bfloat16 [8, 4096, 512], P('pipe', 'ctx'), may hold values from -8 to 8
- keyval: bfloat16 [8, 4096, 256], P('pipe', 'ctx'), may hold values from -8 to 8
- w_qkv: bfloat16 [8, 8192, 768], P('pipe', 'ctx'), may hold values from -0.0625 to 0.0625
- w_out: bfloat16 [8, 8192, 512], P('pipe', 'ctx'), may hold values from -0.25 to 0.25
- doc_lengths: int32 [8, 8], P('pipe'), may hold values from 1 to 2048, 4096 in all within a row
- order: int32 [8, 32], P('pipe'), may hold values from 0 to 31, as said below
Outputs:
- passed_grad: bfloat16 [8, 4096, 8192], P('pipe', 'ctx')
Inputs may be any that keep to these rules, and one draw needn't show every extreme that they name: Each row of order is a permutation of 0 to 31; entry d * 2 + k (device d's stored slot k, k < 2) names one of the sequence blocks e * 2 to e * 2 + 1 of device e = (d + k * 8) mod 16. `doc_lengths`: each row sums to 4096 and its largest entry is 2048.
All inputs are finite; a program needn't handle non-finite values.
Results may differ from a plain program's by a relative error of at most 0.015.
Values may be sent and summed in bfloat16 or wider, within the bound.
No kernel may reach another device: no remote copies, remote signals or barrier semaphores. Data moves between devices by JAX's collectives and lax.ppermute only.
A program may use at most 128 MiB of HBM per device.

v0:
```python
import math
import jax
import jax.numpy as jnp
from jax import lax
from jax.sharding import PartitionSpec as P

BLOCK = 128
ROPE_BASE = 500000.0
MASKED = -1e30


def passed_along(value, axis, steps):
    count = lax.axis_size(axis)
    pairs = [(source, (source + steps) % count) for source in range(count)]
    return lax.ppermute(value, axis, pairs)


def passed_along_2(value, axis, by):
    size = lax.axis_size(axis)
    pairs = [(i, i + by) for i in range(size) if 0 <= i + by < size]
    return lax.ppermute(value, axis, pairs)


def rope_tables(positions, head_dim):
    half_width = head_dim // 2
    inv_freq = ROPE_BASE ** (-(jnp.arange(half_width, dtype=jnp.float32) * 2.0 / head_dim))
    angles = positions.astype(jnp.float32)[:, None] * inv_freq[None, :]
    angles = jnp.concatenate([angles, angles], axis=1)
    return (jnp.cos(angles), jnp.sin(angles))


def unrotate(gradient, positions):
    cosine, sine_table = rope_tables(positions, gradient.shape[1])
    half_width = gradient.shape[1] // 2
    turned = jnp.concatenate([-gradient[:, half_width:], gradient[:, :half_width]], axis=1)
    return gradient * cosine - turned * sine_table


def doc_ids(positions, lengths):
    doc_ends = jnp.cumsum(lengths)[:-1]
    return jnp.sum((positions[:, None] >= doc_ends[None, :]).astype(jnp.int32), axis=1)


def seq_to_stored(rows, block_order, device, ctx_size, per_device):
    width = rows.shape[1]
    first_block = device * per_device
    blocks = rows.reshape(per_device, BLOCK, width)
    pieces = []
    for slot_k in range(per_device):
        offset = slot_k * ctx_size // per_device
        slot_at = (device - offset) % ctx_size * per_device + slot_k
        local_index = block_order[slot_at] - first_block
        chosen = lax.dynamic_index_in_dim(blocks, local_index, 0, keepdims=False)
        if slot_k > 0:
            chosen = passed_along(chosen, "ctx", -offset)
        pieces.append(chosen)
    return jnp.concatenate(pieces, axis=0)


def stored_to_seq(rows, block_order, device, ctx_size, per_device):
    width = rows.shape[1]
    first_block = device * per_device
    blocks = rows.reshape(per_device, BLOCK, width)
    pieces = []
    local_ids = []
    for slot_k in range(per_device):
        offset = slot_k * ctx_size // per_device
        piece = blocks[slot_k]
        if slot_k > 0:
            piece = passed_along(piece, "ctx", offset)
        pieces.append(piece)
        sender_slot = (device - offset) % ctx_size * per_device + slot_k
        local_ids.append(block_order[sender_slot] - first_block)
    stacked = jnp.stack(pieces)
    index_list = jnp.stack(local_ids)
    choose = (jnp.arange(per_device, dtype=jnp.int32)[:, None] == index_list[None, :]).astype(
        rows.dtype
    )
    placed = jnp.einsum("pk,kbw->pbw", choose, stacked, preferred_element_type=jnp.float32)
    return placed.astype(rows.dtype).reshape(-1, width)


def contract_rows(left_rows, right_rows):
    return lax.dot_general(
        left_rows, right_rows, (((0,), (0,)), ((), ())), preferred_element_type=jnp.float32
    )


def contract_cols(left_rows, right_rows):
    return lax.dot_general(
        left_rows, right_rows, (((1,), (1,)), ((), ())), preferred_element_type=jnp.float32
    )


def block_scores(query_rows, key_rows, query_pos, query_doc, key_pos, key_doc, score_scale):
    scores = contract_cols(query_rows, key_rows) * score_scale
    visible = (query_doc[:, None] == key_doc[None, :]) & (key_pos[None, :] <= query_pos[:, None])
    return (scores, visible)


def body(grad_in, query, keyval, w_qkv, w_out, doc_lengths, order):
    section_grad_in = grad_in[0]
    stored_query = query[0]
    stored_keyval = keyval[0]
    in_weight = w_qkv[0]
    out_weight = w_out[0]
    lengths = doc_lengths[0]
    block_order = order[0]
    ctx_size = lax.axis_size("ctx")
    device = lax.axis_index("ctx")
    local_rows = section_grad_in.shape[0]
    head_dim = stored_keyval.shape[1] // 2
    group = stored_query.shape[1] // head_dim
    per_device = local_rows // BLOCK
    block_count = block_order.shape[0]
    seq_len = local_rows * ctx_size
    first_row = device * local_rows
    score_scale = 1.0 / math.sqrt(head_dim)
    key_block = math.gcd(seq_len, 512)
    key_steps = seq_len // key_block
    within = jnp.arange(BLOCK, dtype=jnp.int32)
    out_grad = jnp.dot(
        section_grad_in,
        lax.all_gather(out_weight, "ctx", axis=0, tiled=True),
        preferred_element_type=jnp.float32,
    ).astype(jnp.bfloat16)
    local_out_grad = seq_to_stored(out_grad, block_order, device, ctx_size, per_device)
    query_positions = (block_order[:, None] * BLOCK + within[None, :]).reshape(-1)
    gathered = lax.all_gather(stored_keyval, "ctx", axis=0, tiled=True)
    slot_ids = jnp.arange(block_count, dtype=jnp.int32)
    inverse = jnp.sum(
        jnp.where(block_order[None, :] == slot_ids[:, None], slot_ids[None, :], 0), axis=1
    )
    all_keyval = gathered.reshape(block_count, BLOCK, 2 * head_dim)[inverse].reshape(
        seq_len, 2 * head_dim
    )
    key_positions = jnp.arange(seq_len, dtype=jnp.int32)
    key_docs = doc_ids(key_positions, lengths)
    query_pos = lax.dynamic_slice_in_dim(query_positions, first_row, local_rows)
    query_doc = doc_ids(query_pos, lengths)
    flat_rows = local_rows * group
    flat_query = stored_query.reshape(flat_rows, head_dim)
    flat_grad = local_out_grad.reshape(flat_rows, head_dim)
    flat_pos = jnp.repeat(query_pos, group)
    flat_doc = jnp.repeat(query_doc, group)
    key_blocks = (
        all_keyval.reshape(key_steps, key_block, 2 * head_dim),
        key_positions.reshape(key_steps, key_block),
        key_docs.reshape(key_steps, key_block),
    )

    def running_total(carried, current):
        row_top, row_total, weighted = carried
        pair_rows, key_pos, key_doc = current
        scores, visible = block_scores(
            flat_query, pair_rows[:, :head_dim], flat_pos, flat_doc, key_pos, key_doc, score_scale
        )
        new_top = jnp.maximum(row_top, jnp.max(jnp.where(visible, scores, MASKED), axis=1))
        rescale = jnp.exp(row_top - new_top)
        weights = jnp.where(visible, jnp.exp(scores - new_top[:, None]), 0.0)
        row_total = row_total * rescale + jnp.sum(weights, axis=1)
        value_wide = pair_rows[:, head_dim:].astype(jnp.float32)
        weighted = weighted * rescale[:, None] + jnp.dot(
            weights, value_wide, precision=lax.Precision.HIGHEST
        )
        return ((new_top, row_total, weighted), None)

    start_top = jnp.full((flat_rows,), MASKED, jnp.float32)
    start_carry = (
        start_top,
        jnp.zeros((flat_rows,), jnp.float32),
        jnp.zeros((flat_rows, head_dim), jnp.float32),
    )
    (row_top, row_total, weighted), unused = lax.scan(running_total, start_carry, key_blocks)
    log_total = row_top + jnp.log(row_total)
    attn_out = weighted / row_total[:, None]
    row_delta = jnp.sum(flat_grad.astype(jnp.float32) * attn_out, axis=1)

    def grad_step(summed, current):
        pair_rows, key_pos, key_doc = current
        scores, visible = block_scores(
            flat_query, pair_rows[:, :head_dim], flat_pos, flat_doc, key_pos, key_doc, score_scale
        )
        attn_prob = jnp.where(visible, jnp.exp(scores - log_total[:, None]), 0.0)
        prob_grad = contract_cols(flat_grad, pair_rows[:, head_dim:])
        score_grad = (score_scale * attn_prob * (prob_grad - row_delta[:, None])).astype(
            jnp.bfloat16
        )
        summed = summed + jnp.dot(
            score_grad, pair_rows[:, :head_dim], preferred_element_type=jnp.float32
        )
        key_term = contract_rows(score_grad, flat_query)
        value_term = contract_rows(attn_prob.astype(jnp.bfloat16), flat_grad)
        return (summed, jnp.concatenate([key_term, value_term], axis=1))

    query_grad_rot, key_terms = lax.scan(
        grad_step, jnp.zeros((flat_rows, head_dim), jnp.float32), key_blocks
    )
    own_positions = first_row + jnp.arange(local_rows, dtype=jnp.int32)
    keyval_grad = lax.psum_scatter(
        key_terms.reshape(seq_len, 2 * head_dim).astype(jnp.bfloat16),
        "ctx",
        scatter_dimension=0,
        tiled=True,
    ).astype(jnp.float32)
    query_grad = (
        unrotate(query_grad_rot, flat_pos)
        .reshape(local_rows, group * head_dim)
        .astype(jnp.bfloat16)
    )
    query_grad = stored_to_seq(query_grad, block_order, device, ctx_size, per_device)
    key_grad = unrotate(keyval_grad[:, :head_dim], own_positions).astype(jnp.bfloat16)
    value_grad = keyval_grad[:, head_dim:].astype(jnp.bfloat16)
    qkv_grad = jnp.concatenate([query_grad, key_grad, value_grad], axis=1)
    projected = contract_cols(qkv_grad, lax.all_gather(in_weight, "ctx", axis=0, tiled=True))
    section_grad = (section_grad_in.astype(jnp.float32) + projected).astype(jnp.bfloat16)
    passed = passed_along_2(section_grad, "pipe", -1)
    return passed[None]


def solution(mesh):
    return jax.shard_map(
        body,
        mesh=mesh,
        in_specs=(
            P("pipe", "ctx", None),
            P("pipe", "ctx", None),
            P("pipe", "ctx", None),
            P("pipe", "ctx", None),
            P("pipe", "ctx", None),
            P("pipe", None),
            P("pipe", None),
        ),
        out_specs=P("pipe", "ctx", None),
        check_vma=False,
    )
```

profile of v0, /device:TPU:1, one launch (start us, length us, event | category | flops | bytes accessed | tf_op | source)
XLA Modules:
  0.0 424.1 jit_solution(3476864368131219313)
XLA Ops:
  8.1 1.3 constant_dynamic-slice_fusion.5
  10.7 0.8 reduce-window.4
  11.6 1.1 reshape_squeeze.3
  14.5 42.2 %all-gather.7.cloned.1.call-done = bf16[1,4096,256]{2,1,0:T(8,128)(2,1)} async-done(((bf16[1,256,256]{2,1,0:T(8,128)(2,1)}), bf16[1,4096,256]{2,1,0:T(8,128)(2,1)}) %all-gather.7.cloned.1.call-update) | async-done | bytes 2097168 | tf_op jit(solution)/shard_map/all_gather | solution.py:129
  56.7 3.6 gather_fusion
  60.3 51.0 %while.28 = (s32[]{:T(128)}, f32[1024]{0:T(1024)S(1)}, f32[1024]{0:T(1024)S(1)}, f32[1024,128]{1,0:T(8,128)}, s32[8,512]{1,0:T(8,128)S(1)}, /*index=5*/s32[8,512...) while((s32[]{:T(128)}, f32[1024]{0:T(1024)S(1)}, ...), condition=%wide.region_7.8_spmd.clone, body=%wide.region_4.7_spmd.clone.sunk | while | flops 949883904 | bytes 12720321 | solution.py:174
  60.3 1.0 dynamic-slice_bitcast_fusion.6
  63.4 2.4 convolution_add_fusion.4
  65.9 0.8 copy-done.1
  66.7 1.0 dynamic-slice_bitcast_fusion.6
  69.8 2.4 convolution_add_fusion.4
  73.1 1.0 dynamic-slice_bitcast_fusion.6
  76.2 2.4 convolution_add_fusion.4
  79.5 1.0 dynamic-slice_bitcast_fusion.6
  82.6 2.4 convolution_add_fusion.4
  85.8 1.0 dynamic-slice_bitcast_fusion.6
  88.9 2.4 convolution_add_fusion.4
  92.2 1.1 dynamic-slice_bitcast_fusion.6
  95.3 2.4 convolution_add_fusion.4
  98.6 1.0 dynamic-slice_bitcast_fusion.6
  101.7 2.4 convolution_add_fusion.4
  104.9 1.0 dynamic-slice_bitcast_fusion.6
  108.0 2.4 convolution_add_fusion.4
  111.3 18.4 %all-gather.9.cloned.1.call-done = bf16[1,8192,512]{2,1,0:T(8,128)(2,1)} async-done(((bf16[1,512,512]{2,1,0:T(8,128)(2,1)}), bf16[1,8192,512]{2,1,0:T(8,128)(2,1)}) %all-gather.9.cloned.1.call-update) | async-done | bytes 8388624 | tf_op jit(solution)/shard_map/all_gather | solution.py:124
  129.7 7.0 %fusion.43 = bf16[256,512]{1,0:T(8,128)(2,1)S(1)} fusion(bf16[1,8192,512]{2,1,0:T(8,128)(2,1)} %all-gather.9.cloned.1.call-done, bf16[1,256,8192]{2,1,0:T(8,128)(2,1)} %param.11), kind=kOutput, calls=%fused_computation.55 | convolution fusion | flops 2147614720 | bytes 12845056 | tf_op jit(solution)/shard_map/dot_general | solution.py:122
  136.7 2.8 collective-permute-start
  139.5 3.2 collective-permute-done
  143.3 41.0 %while.29 = (s32[]{:T(128)}, f32[1024,128]{1,0:T(8,128)S(1)}, bf16[8,512,256]{2,1,0:T(8,128)(2,1)}, s32[8,512]{1,0:T(8,128)S(1)}, s32[8,512]{1,0:T(8,128)S(1)}, ...) while((s32[]{:T(128)}, f32[1024,128]{1,0:T(8,128)S(1)}, ...), condition=%wide.region_10.11_spmd.clone, body=%wide.region_9.10_spmd.clone.sunk | while | flops 677642240 | bytes 14342807 | solution.py:196
  143.3 1.0 dynamic-slice_bitcast_fusion.7
  148.4 1.0 dynamic-slice_bitcast_fusion.7
  153.5 1.0 dynamic-slice_bitcast_fusion.7
  158.7 1.0 dynamic-slice_bitcast_fusion.7
  163.8 1.0 dynamic-slice_bitcast_fusion.7
  168.9 1.0 dynamic-slice_bitcast_fusion.7
  174.0 1.0 dynamic-slice_bitcast_fusion.7
  179.2 1.0 dynamic-slice_bitcast_fusion.7
  185.6 2.4 fusion.49
  188.1 2.9 collective-permute-start.1
  191.2 2.4 collective-permute-done.1
  194.6 63.0 %reduce-scatter.2.cloned.1.call-done = bf16[256,256]{1,0:T(8,128)(2,1)} async-done(((bf16[4096,256]{1,0:T(8,128)(2,1)}), bf16[256,256]{1,0:T(8,128)(2,1)}) %reduce-scatter.2.cloned.1.call-update) | async-done | bytes 131088 | tf_op jit(solution)/shard_map/reduce_scatter | solution.py:200
  257.6 0.9 convert_element_type.75
  258.5 0.9 slice.79
  259.4 0.8 slice.80
  260.9 89.8 %all-gather.11.cloned.1.call-done = bf16[1,8192,768]{2,1,0:T(8,128)(2,1)} async-done(((bf16[1,512,768]{2,1,0:T(8,128)(2,1)}), bf16[1,8192,768]{2,1,0:T(8,128)(2,1)}) %all-gather.11.cloned.1.call-update) | async-done | bytes 12582928 | tf_op jit(solution)/shard_map/all_gather | solution.py:215
  350.7 14.8 %fusion.37 = bf16[256,8192]{1,0:T(8,128)(2,1)} fusion(bf16[1,8192,768]{2,1,0:T(8,128)(2,1)} %all-gather.11.cloned.1.call-done, bf16[1,256,8192]{2,1,0:T(8,128)(2,1)} %param.11, bf16[256,128]{1,0:T(8,128)(2,1)S(1)} %slice.80, bf16[256,128]{1,0:T(8,128)(2,1)S(1)} %fusion.57, bf16[256,512]{1,0:T(8,128)(2,1)S(1)} %bitcast.123), kind=kOutput, calls=%fused_computation.50 | convolution fusion | flops 3228696576 | bytes 21364736 | tf_op jit(solution)/shard_map/dot_general | solution.py:90
  365.5 2.6 collective-permute-start.2
  368.1 47.5 %collective-permute-done.2 = bf16[256,8192]{1,0:T(8,128)(2,1)S(1)} collective-permute-done((bf16[256,8192]{1,0:T(8,128)(2,1)}, bf16[256,8192]{1,0:T(8,128)(2,1)S(1)}, u32[]{:S(2)}, u32[]{:S(2)}) %collective-permute-start.2) | collective-permute-done | bytes 4194336 | tf_op jit(solution)/shard_map/ppermute | solution.py:21
  415.6 2.0 copy.44
  (262 shorter events, 61.7 us)
Async XLA Ops:
  6.5 50.2 %all-gather.7.cloned.1.call-start = ((), (), s32[]{:S(2)}) async-start(), calls=%async_computation.2 | async-start | bytes 2228224 | tf_op jit(solution)/shard_map/all_gather | solution.py:129
  7.3 122.5 %all-gather.9.cloned.1.call-start = ((), (), s32[]{:S(2)}) async-start(), calls=%async_computation.3 | async-start | bytes 8912896 | tf_op jit(solution)/shard_map/all_gather | solution.py:124
  8.0 249.6 %reduce-scatter.2.cloned.1.call-start = ((), (), s32[]{:S(2)}) async-start(), calls=%async_computation.1 | async-start | bytes 2228224 | tf_op jit(solution)/shard_map/reduce_scatter | solution.py:200
  62.4 1.0 copy-start
  65.9 0.8 copy-start.1
  68.8 1.1 copy-start
  72.3 0.8 copy-start.1
  75.1 1.1 copy-start
  78.6 0.8 copy-start.1
  81.5 1.0 copy-start
  85.0 0.8 copy-start.1
  87.9 1.0 copy-start
  91.3 0.8 copy-start.1
  94.3 1.0 copy-start
  97.8 0.8 copy-start.1
  100.6 1.0 copy-start
  104.1 0.8 copy-start.1
  107.0 1.0 copy-start
  110.5 0.8 copy-start.1
  111.3 31.6 %copy-start.2 = (f32[1024,128]{1,0:T(8,128)S(1)}, f32[1024,128]{1,0:T(8,128)}, u32[]{:S(2)}) copy-start(f32[1024,128]{1,0:T(8,128)} %get-tuple-element.124) | copy-start | bytes 1572868
  136.7 5.9 %collective-permute-start = (bf16[128,512]{1,0:T(8,128)(2,1)S(1)}, bf16[128,512]{1,0:T(8,128)(2,1)S(1)}, u32[]{:S(2)}, u32[]{:S(2)}) collective-permute-start(bf16[128,512]{1,0:T(8,128)(2,1)S(1)} %get-tuple-element.270), channel_id=1, source_target_pairs={{0,8},{1,9},{2,10},{3,11},{4,12},{5,13},{6,14},{7,15},{8,0},{9,1},... | collective-permute-start | bytes 393224 | tf_op jit(solution)/shard_map/ppermute | solution.py:15
  184.3 166.3 %all-gather.11.cloned.1.call-start = ((), (), s32[]{:S(2)}) async-start(), calls=%async_computation.4 | async-start | bytes 13369344 | tf_op jit(solution)/shard_map/all_gather | solution.py:215
  188.1 5.6 %collective-permute-start.1 = (bf16[128,512]{1,0:T(8,128)(2,1)S(1)}, bf16[128,512]{1,0:T(8,128)(2,1)S(1)}, u32[]{:S(2)}, u32[]{:S(2)}) collective-permute-start(bf16[128,512]{1,0:T(8,128)(2,1)S(1)} %slice.59), channel_id=1, source_target_pairs={{0,8},{1,9},{2,10},{3,11},{4,12},{5,13},{6,14},{7,15},{8,0},{9,1},... | collective-permute-start | bytes 393224 | tf_op jit(solution)/shard_map/ppermute | solution.py:15
  365.5 50.1 %collective-permute-start.2 = (bf16[256,8192]{1,0:T(8,128)(2,1)}, bf16[256,8192]{1,0:T(8,128)(2,1)S(1)}, u32[]{:S(2)}, u32[]{:S(2)}) collective-permute-start(bf16[256,8192]{1,0:T(8,128)(2,1)} %fusion.37), channel_id=1, source_target_pairs={{16,0},{32,16},{48,32},{64,48},{80,64},{96,80},{112,96},{17,1},{33... | collective-permute-start | bytes 12582920 | tf_op jit(solution)/shard_map/ppermute | solution.py:21
Sparse Core Ops, SparseCore 0:
  9.5 47.1 all-gather.6
  58.8 70.8 all-gather.8
  184.4 73.1 reduce-scatter.1
  259.8 90.8 all-gather.10
where the time goes:
time: 425 us; the launch traced here: 424 us
  waiting for transfers between devices  269 us (63%)
  matrix products  68.8 us (16%)
  local copies, waits for them, and re-layouts  49.3 us (12%)
  between operations  14.6 us (3%)
  other arithmetic  13 us (3%)
  starting transfers between devices  8.38 us (2%)
    all_gather x1, waiting for transfers between devices, body(): lax.all_gather(in_weight, 'ctx', axis=0, tiled=True)  89.8 us
    reduce_scatter x1, waiting for transfers between devices, body(): lax.psum_scatter(key_terms.reshape(seq_len, 2 * head_dim).astype(jnp.bflo...  63 us
    ppermute x1, waiting for transfers between devices, passed_along_2(): return lax.ppermute(value, axis, pairs)  47.5 us
    all_gather x1, waiting for transfers between devices, body(): gathered = lax.all_gather(stored_keyval, 'ctx', axis=0, tiled=True)  42.2 us
    dot_general x25, matrix products, contract_cols(): lax.dot_general(left_rows, right_rows, (((1,), (1,)), ((), ())), preferre...  29.2 us
    dot_general x8, matrix products, running_total(): jnp.dot(weights, value_wide, precision=lax.Precision.HIGHEST)  19.4 us
    all_gather x1, waiting for transfers between devices, body(): lax.all_gather(out_weight, 'ctx', axis=0, tiled=True)  18.4 us
    squeeze x16, local copies, waits for them, and re-layouts, body(): lax.scan(running_total, start_carry, key_blocks)  15.7 us
  transfers between devices with their start and end apart: 7, of which 7 were waited for; matrix products, arithmetic and copies ran while one was open for 13% of the time, Pallas kernels for 0%

commit v1 on v0

--- a/solution.py
+++ b/solution.py
@@ -1,3 +1,4 @@
+import functools
 import math
 import jax
 import jax.numpy as jnp
@@ -7,6 +8,25 @@
 BLOCK = 128
 ROPE_BASE = 500000.0
 MASKED = -1e30
+
+
+def scenes_test(buf, along_dim):
+    n_lanes = lax.axis_size("ctx")
+    row_list = [buf]
+    jj = 0
+    while jj < n_lanes - 1:
+        row_list.append(
+            lax.ppermute(row_list[-1], "ctx", [(t, (t + 1) % n_lanes) for t in range(n_lanes)])
+        )
+        jj += 1
+    return jnp.roll(
+        jnp.concatenate(row_list[::-1], along_dim),
+        (lax.axis_index("ctx") + 1) * buf.shape[along_dim],
+        along_dim,
+    )
+
+
+mix_the_zone = functools.partial(scenes_test, along_dim=0)
 
 
 def passed_along(value, axis, steps):
@@ -126,7 +146,7 @@
     ).astype(jnp.bfloat16)
     local_out_grad = seq_to_stored(out_grad, block_order, device, ctx_size, per_device)
     query_positions = (block_order[:, None] * BLOCK + within[None, :]).reshape(-1)
-    gathered = lax.all_gather(stored_keyval, "ctx", axis=0, tiled=True)
+    gathered = mix_the_zone(stored_keyval)
     slot_ids = jnp.arange(block_count, dtype=jnp.int32)
     inverse = jnp.sum(
         jnp.where(block_order[None, :] == slot_ids[:, None], slot_ids[None, :], 0), axis=1

time: 425 us -> 495 us (1.16)
  waiting for transfers between devices: 269 us -> 341 us
  matrix products: 68.8 us -> 80.4 us
  local copies, waits for them, and re-layouts: 49.3 us -> 38.8 us
    ppermute x0 -> x15, waiting for transfers between devices: none -> 110 us  [scenes_test(): lax.ppermute(row_list[-1], 'ctx', [(t, (t + 1) % n_lanes) for t in range(...]
    all_gather x1 -> x0, waiting for transfers between devices: 42.2 us -> none  [body(): gathered = lax.all_gather(stored_keyval, 'ctx', axis=0, tiled=True)]
    reduce_scatter x1, waiting for transfers between devices: 63 us -> 82.2 us  [body(): lax.psum_scatter(key_terms.reshape(seq_len, 2 * head_dim).astype(jnp.bflo...]
    all_gather x1, waiting for transfers between devices: 18.4 us -> 0.01 us  [body(): lax.all_gather(out_weight, 'ctx', axis=0, tiled=True)]
    dot_general x8, matrix products: 19.4 us -> 31.2 us  [running_total(): jnp.dot(weights, value_wide, precision=lax.Precision.HIGHEST)]
    while x40 -> x8, local copies, waits for them, and re-layouts: 9.41 us -> 0.01 us
    ppermute x2, starting transfers between devices: 5.69 us -> 0.39 us  [passed_along(): return lax.ppermute(value, axis, pairs)]
  transfers between devices with their start and end apart: 7 -> 21, of which waited for: 7 -> 20; matrix products, arithmetic and copies ran while one was open for 13% -> 14% of each run, Pallas kernels for 0% -> 0%
where the time goes in v1:
time: 495 us; the launch traced here: 494 us
  waiting for transfers between devices  341 us (69%)
  matrix products  80.4 us (16%)
  local copies, waits for them, and re-layouts  38.8 us (8%)
  between operations  15 us (3%)
  other arithmetic  13 us (3%)
  starting transfers between devices  5.12 us (1%)
    ppermute x15, waiting for transfers between devices, scenes_test(): lax.ppermute(row_list[-1], 'ctx', [(t, (t + 1) % n_lanes) for t in range(...  110 us
    all_gather x1, waiting for transfers between devices, body(): lax.all_gather(in_weight, 'ctx', axis=0, tiled=True)  89.9 us
    reduce_scatter x1, waiting for transfers between devices, body(): lax.psum_scatter(key_terms.reshape(seq_len, 2 * head_dim).astype(jnp.bflo...  82.2 us
    ppermute x1, waiting for transfers between devices, passed_along_2(): return lax.ppermute(value, axis, pairs)  47.5 us
    dot_general x8, matrix products, running_total(): jnp.dot(weights, value_wide, precision=lax.Precision.HIGHEST)  31.2 us
    dot_general x25, matrix products, contract_cols(): lax.dot_general(left_rows, right_rows, (((1,), (1,)), ((), ())), preferre...  29.1 us
    squeeze x16, local copies, waits for them, and re-layouts, body(): lax.scan(running_total, start_carry, key_blocks)  15.6 us
    ppermute x2, waiting for transfers between devices, passed_along(): return lax.ppermute(value, axis, pairs)  10.4 us
  transfers between devices with their start and end apart: 21, of which 20 were waited for; matrix products, arithmetic and copies ran while one was open for 14% of the time, Pallas kernels for 0%

profile of v1, /device:TPU:1, one launch (start us, length us, event | category | flops | bytes accessed | tf_op | source)
XLA Modules:
  0.0 494.3 jit_solution(2750978173943727231)
XLA Ops:
  6.5 2.0 collective-permute-start
  8.6 7.2 %collective-permute-done = bf16[256,256]{1,0:T(8,128)(2,1)S(1)} collective-permute-done((bf16[256,256]{1,0:T(8,128)(2,1)}, bf16[256,256]{1,0:T(8,128)(2,1)S(1)}, u32[]{:S(2)}, u32[]{:S(2)}) %collective-permute-start) | collective-permute-done | bytes 131104 | tf_op jit(solution)/shard_map/ppermute | solution.py:19
  15.8 7.1 %collective-permute-done.1 = bf16[256,256]{1,0:T(8,128)(2,1)S(1)} collective-permute-done((bf16[256,256]{1,0:T(8,128)(2,1)S(1)}, bf16[256,256]{1,0:T(8,128)(2,1)S(1)}, u32[]{:S(2)}, u32[]{:S(2)}) %collective-permute-start.1) | collective-permute-done | bytes 131104 | tf_op jit(solution)/shard_map/ppermute | solution.py:19
  22.9 7.1 %collective-permute-done.2 = bf16[256,256]{1,0:T(8,128)(2,1)S(1)} collective-permute-done((bf16[256,256]{1,0:T(8,128)(2,1)S(1)}, bf16[256,256]{1,0:T(8,128)(2,1)S(1)}, u32[]{:S(2)}, u32[]{:S(2)}) %collective-permute-start.2) | collective-permute-done | bytes 131104 | tf_op jit(solution)/shard_map/ppermute | solution.py:19
  30.1 7.1 %collective-permute-done.3 = bf16[256,256]{1,0:T(8,128)(2,1)S(1)} collective-permute-done((bf16[256,256]{1,0:T(8,128)(2,1)S(1)}, bf16[256,256]{1,0:T(8,128)(2,1)S(1)}, u32[]{:S(2)}, u32[]{:S(2)}) %collective-permute-start.3) | collective-permute-done | bytes 131104 | tf_op jit(solution)/shard_map/ppermute | solution.py:19
  37.2 7.1 %collective-permute-done.4 = bf16[256,256]{1,0:T(8,128)(2,1)S(1)} collective-permute-done((bf16[256,256]{1,0:T(8,128)(2,1)S(1)}, bf16[256,256]{1,0:T(8,128)(2,1)S(1)}, u32[]{:S(2)}, u32[]{:S(2)}) %collective-permute-start.4) | collective-permute-done | bytes 131104 | tf_op jit(solution)/shard_map/ppermute | solution.py:19
  44.4 7.1 %collective-permute-done.5 = bf16[256,256]{1,0:T(8,128)(2,1)S(1)} collective-permute-done((bf16[256,256]{1,0:T(8,128)(2,1)S(1)}, bf16[256,256]{1,0:T(8,128)(2,1)S(1)}, u32[]{:S(2)}, u32[]{:S(2)}) %collective-permute-start.5) | collective-permute-done | bytes 131104 | tf_op jit(solution)/shard_map/ppermute | solution.py:19
  51.5 7.7 %collective-permute-done.6 = bf16[256,256]{1,0:T(8,128)(2,1)S(1)} collective-permute-done((bf16[256,256]{1,0:T(8,128)(2,1)S(1)}, bf16[256,256]{1,0:T(8,128)(2,1)S(1)}, u32[]{:S(2)}, u32[]{:S(2)}) %collective-permute-start.6) | collective-permute-done | bytes 131104 | tf_op jit(solution)/shard_map/ppermute | solution.py:19
  59.2 8.5 %collective-permute-done.7 = bf16[256,256]{1,0:T(8,128)(2,1)S(1)} collective-permute-done((bf16[256,256]{1,0:T(8,128)(2,1)S(1)}, bf16[256,256]{1,0:T(8,128)(2,1)S(1)}, u32[]{:S(2)}, u32[]{:S(2)}) %collective-permute-start.7) | collective-permute-done | bytes 131104 | tf_op jit(solution)/shard_map/ppermute | solution.py:19
  67.8 7.6 %collective-permute-done.8 = bf16[256,256]{1,0:T(8,128)(2,1)S(1)} collective-permute-done((bf16[256,256]{1,0:T(8,128)(2,1)S(1)}, bf16[256,256]{1,0:T(8,128)(2,1)S(1)}, u32[]{:S(2)}, u32[]{:S(2)}) %collective-permute-start.8) | collective-permute-done | bytes 131104 | tf_op jit(solution)/shard_map/ppermute | solution.py:19
  76.0 6.5 %collective-permute-done.9 = bf16[256,256]{1,0:T(8,128)(2,1)S(1)} collective-permute-done((bf16[256,256]{1,0:T(8,128)(2,1)S(1)}, bf16[256,256]{1,0:T(8,128)(2,1)S(1)}, u32[]{:S(2)}, u32[]{:S(2)}) %collective-permute-start.9) | collective-permute-done | bytes 131104 | tf_op jit(solution)/shard_map/ppermute | solution.py:19
  84.2 5.5 %collective-permute-done.10 = bf16[256,256]{1,0:T(8,128)(2,1)S(1)} collective-permute-done((bf16[256,256]{1,0:T(8,128)(2,1)S(1)}, bf16[256,256]{1,0:T(8,128)(2,1)S(1)}, u32[]{:S(2)}, u32[]{:S(2)}) %collective-permute-start.10) | collective-permute-done | bytes 131104 | tf_op jit(solution)/shard_map/ppermute | solution.py:19
  89.6 9.6 %collective-permute-done.11 = bf16[256,256]{1,0:T(8,128)(2,1)S(1)} collective-permute-done((bf16[256,256]{1,0:T(8,128)(2,1)S(1)}, bf16[256,256]{1,0:T(8,128)(2,1)S(1)}, u32[]{:S(2)}, u32[]{:S(2)}) %collective-permute-start.11) | collective-permute-done | bytes 131104 | tf_op jit(solution)/shard_map/ppermute | solution.py:19
  99.2 8.1 %collective-permute-done.12 = bf16[256,256]{1,0:T(8,128)(2,1)S(1)} collective-permute-done((bf16[256,256]{1,0:T(8,128)(2,1)S(1)}, bf16[256,256]{1,0:T(8,128)(2,1)S(1)}, u32[]{:S(2)}, u32[]{:S(2)}) %collective-permute-start.12) | collective-permute-done | bytes 131104 | tf_op jit(solution)/shard_map/ppermute | solution.py:19
  107.4 7.0 %collective-permute-done.13 = bf16[256,256]{1,0:T(8,128)(2,1)S(1)} collective-permute-done((bf16[256,256]{1,0:T(8,128)(2,1)S(1)}, bf16[256,256]{1,0:T(8,128)(2,1)S(1)}, u32[]{:S(2)}, u32[]{:S(2)}) %collective-permute-start.13) | collective-permute-done | bytes 131104 | tf_op jit(solution)/shard_map/ppermute | solution.py:19
  114.5 1.4 constant_dynamic-slice_fusion.6
  117.3 1.1 reshape_squeeze.3
  118.5 6.6 %collective-permute-done.14 = bf16[256,256]{1,0:T(8,128)(2,1)S(1)} collective-permute-done((bf16[256,256]{1,0:T(8,128)(2,1)S(1)}, bf16[256,256]{1,0:T(8,128)(2,1)S(1)}, u32[]{:S(2)}, u32[]{:S(2)}) %collective-permute-start.14) | collective-permute-done | bytes 131104 | tf_op jit(solution)/shard_map/ppermute | solution.py:19
  125.9 2.0 gather_fusion
  128.0 53.0 %while.28 = (s32[]{:T(128)}, f32[1024]{0:T(1024)S(1)}, f32[1024]{0:T(1024)S(1)}, f32[1024,128]{1,0:T(8,128)}, s32[8,512]{1,0:T(8,128)S(1)}, /*index=5*/s32[8,512...) while((s32[]{:T(128)}, f32[1024]{0:T(1024)S(1)}, ...), condition=%wide.region_7.8_spmd.clone, body=%wide.region_4.7_spmd.clone.sunk | while | flops 949883904 | bytes 8525961 | solution.py:194
  128.0 1.0 dynamic-slice_bitcast_fusion.6
  130.7 3.0 convolution_add_fusion.4
  133.7 1.0 dynamic-slice_bitcast_fusion.6
  136.4 4.0 convolution_add_fusion.4
  140.5 1.0 dynamic-slice_bitcast_fusion.6
  143.2 4.0 convolution_add_fusion.4
  147.2 1.0 dynamic-slice_bitcast_fusion.6
  149.9 4.0 convolution_add_fusion.4
  154.0 1.0 dynamic-slice_bitcast_fusion.6
  156.7 4.0 convolution_add_fusion.4
  160.7 1.0 dynamic-slice_bitcast_fusion.6
  163.5 4.0 convolution_add_fusion.4
  167.5 1.0 dynamic-slice_bitcast_fusion.6
  170.2 4.0 convolution_add_fusion.4
  174.2 1.0 dynamic-slice_bitcast_fusion.6
  177.0 4.0 convolution_add_fusion.4
  181.0 7.0 %fusion.43 = bf16[256,512]{1,0:T(8,128)(2,1)S(1)} fusion(bf16[1,8192,512]{2,1,0:T(8,128)(2,1)} %all-gather.5.cloned.1.call-done, bf16[1,256,8192]{2,1,0:T(8,128)(2,1)} %param.11), kind=kOutput, calls=%fused_computation.55 | convolution fusion | flops 2147614720 | bytes 12845056 | tf_op jit(solution)/shard_map/dot_general | solution.py:142
  188.2 5.3 %collective-permute-done.15 = bf16[128,512]{1,0:T(8,128)(2,1)S(1)} collective-permute-done((bf16[128,512]{1,0:T(8,128)(2,1)S(1)}, bf16[128,512]{1,0:T(8,128)(2,1)S(1)}, u32[]{:S(2)}, u32[]{:S(2)}) %collective-permute-start.15) | collective-permute-done | bytes 131104 | tf_op jit(solution)/shard_map/ppermute | solution.py:35
  194.0 40.8 %while.29 = (s32[]{:T(128)}, f32[1024,128]{1,0:T(8,128)S(1)}, bf16[8,512,256]{2,1,0:T(8,128)(2,1)}, s32[8,512]{1,0:T(8,128)S(1)}, s32[8,512]{1,0:T(8,128)S(1)}, ...) while((s32[]{:T(128)}, f32[1024,128]{1,0:T(8,128)S(1)}, ...), condition=%wide.region_10.11_spmd.clone, body=%wide.region_9.10_spmd.clone.sunk | while | flops 677642240 | bytes 14342807 | solution.py:216
  194.1 1.0 dynamic-slice_bitcast_fusion.7
  236.3 2.4 fusion.49
  239.3 5.1 %collective-permute-done.16 = bf16[128,512]{1,0:T(8,128)(2,1)S(1)} collective-permute-done((bf16[128,512]{1,0:T(8,128)(2,1)S(1)}, bf16[128,512]{1,0:T(8,128)(2,1)S(1)}, u32[]{:S(2)}, u32[]{:S(2)}) %collective-permute-start.16) | collective-permute-done | bytes 131104 | tf_op jit(solution)/shard_map/ppermute | solution.py:35
  245.4 82.2 %reduce-scatter.2.cloned.1.call-done = bf16[256,256]{1,0:T(8,128)(2,1)} async-done(((bf16[4096,256]{1,0:T(8,128)(2,1)}), bf16[256,256]{1,0:T(8,128)(2,1)}) %reduce-scatter.2.cloned.1.call-update) | async-done | bytes 131088 | tf_op jit(solution)/shard_map/reduce_scatter | solution.py:220
  330.9 89.9 %all-gather.7.cloned.1.call-done = bf16[1,8192,768]{2,1,0:T(8,128)(2,1)} async-done(((bf16[1,512,768]{2,1,0:T(8,128)(2,1)}), bf16[1,8192,768]{2,1,0:T(8,128)(2,1)}) %all-gather.7.cloned.1.call-update) | async-done | bytes 12582928 | tf_op jit(solution)/shard_map/all_gather | solution.py:235
  420.8 14.8 %fusion.37 = bf16[256,8192]{1,0:T(8,128)(2,1)} fusion(bf16[1,8192,768]{2,1,0:T(8,128)(2,1)} %all-gather.7.cloned.1.call-done, bf16[1,256,8192]{2,1,0:T(8,128)(2,1)} %param.11, bf16[256,128]{1,0:T(8,128)(2,1)S(1)} %slice.80, bf16[256,128]{1,0:T(8,128)(2,1)S(1)} %fusion.57, bf16[256,512]{1,0:T(8,128)(2,1)S(1)} %bitcast.127), kind=kOutput, calls=%fused_computation.50 | convolution fusion | flops 3228696576 | bytes 21364736 | tf_op jit(solution)/shard_map/dot_general | solution.py:110
  435.6 2.6 collective-permute-start.17
  438.2 47.5 %collective-permute-done.17 = bf16[256,8192]{1,0:T(8,128)(2,1)S(1)} collective-permute-done((bf16[256,8192]{1,0:T(8,128)(2,1)}, bf16[256,8192]{1,0:T(8,128)(2,1)S(1)}, u32[]{:S(2)}, u32[]{:S(2)}) %collective-permute-start.17) | collective-permute-done | bytes 4194336 | tf_op jit(solution)/shard_map/ppermute | solution.py:41
  485.8 2.0 copy.75
  (292 shorter events, 62.7 us)
Async XLA Ops:
  6.5 118.9 %copy-start.1 = (bf16[1,256,256]{2,1,0:T(8,128)(2,1)S(1)}, bf16[1,256,256]{2,1,0:T(8,128)(2,1)}, u32[]{:S(2)}) copy-start(bf16[1,256,256]{2,1,0:T(8,128)(2,1)} %param.13) | copy-start | bytes 393220
  6.5 174.5 %all-gather.5.cloned.1.call-start = ((), (), s32[]{:S(2)}) async-start(), calls=%async_computation.2 | async-start | bytes 8912896 | tf_op jit(solution)/shard_map/all_gather | solution.py:144
  6.5 9.3 %collective-permute-start = (bf16[256,256]{1,0:T(8,128)(2,1)}, bf16[256,256]{1,0:T(8,128)(2,1)S(1)}, u32[]{:S(2)}, u32[]{:S(2)}) collective-permute-start(bf16[256,256]{1,0:T(8,128)(2,1)} %bitcast.126), channel_id=1, source_target_pairs={{0,1},{1,2},{2,3},{3,4},{4,5},{5,6},{6,7},{7,8},{8,9},{9,10},{10,1... | collective-permute-start | bytes 393224 | tf_op jit(solution)/shard_map/ppermute | solution.py:19
  15.8 7.1 %collective-permute-start.1 = (bf16[256,256]{1,0:T(8,128)(2,1)S(1)}, bf16[256,256]{1,0:T(8,128)(2,1)S(1)}, u32[]{:S(2)}, u32[]{:S(2)}) collective-permute-start(bf16[256,256]{1,0:T(8,128)(2,1)S(1)} %collective-permute-done), channel_id=1, source_target_pairs={{0,1},{1,2},{2,3},{3,4},{4,5},{5,6},{6,7},{7,8},{8,9},{9,10},{10,1... | collective-permute-start | bytes 393224 | tf_op jit(solution)/shard_map/ppermute | solution.py:19
  22.9 7.1 %collective-permute-start.2 = (bf16[256,256]{1,0:T(8,128)(2,1)S(1)}, bf16[256,256]{1,0:T(8,128)(2,1)S(1)}, u32[]{:S(2)}, u32[]{:S(2)}) collective-permute-start(bf16[256,256]{1,0:T(8,128)(2,1)S(1)} %collective-permute-done.1), channel_id=1, source_target_pairs={{0,1},{1,2},{2,3},{3,4},{4,5},{5,6},{6,7},{7,8},{8,9},{9,10},{10,1... | collective-permute-start | bytes 393224 | tf_op jit(solution)/shard_map/ppermute | solution.py:19
  30.1 7.1 %collective-permute-start.3 = (bf16[256,256]{1,0:T(8,128)(2,1)S(1)}, bf16[256,256]{1,0:T(8,128)(2,1)S(1)}, u32[]{:S(2)}, u32[]{:S(2)}) collective-permute-start(bf16[256,256]{1,0:T(8,128)(2,1)S(1)} %collective-permute-done.2), channel_id=1, source_target_pairs={{0,1},{1,2},{2,3},{3,4},{4,5},{5,6},{6,7},{7,8},{8,9},{9,10},{10,1... | collective-permute-start | bytes 393224 | tf_op jit(solution)/shard_map/ppermute | solution.py:19
  37.2 7.1 %collective-permute-start.4 = (bf16[256,256]{1,0:T(8,128)(2,1)S(1)}, bf16[256,256]{1,0:T(8,128)(2,1)S(1)}, u32[]{:S(2)}, u32[]{:S(2)}) collective-permute-start(bf16[256,256]{1,0:T(8,128)(2,1)S(1)} %collective-permute-done.3), channel_id=1, source_target_pairs={{0,1},{1,2},{2,3},{3,4},{4,5},{5,6},{6,7},{7,8},{8,9},{9,10},{10,1... | collective-permute-start | bytes 393224 | tf_op jit(solution)/shard_map/ppermute | solution.py:19
  44.4 7.1 %collective-permute-start.5 = (bf16[256,256]{1,0:T(8,128)(2,1)S(1)}, bf16[256,256]{1,0:T(8,128)(2,1)S(1)}, u32[]{:S(2)}, u32[]{:S(2)}) collective-permute-start(bf16[256,256]{1,0:T(8,128)(2,1)S(1)} %collective-permute-done.4), channel_id=1, source_target_pairs={{0,1},{1,2},{2,3},{3,4},{4,5},{5,6},{6,7},{7,8},{8,9},{9,10},{10,1... | collective-permute-start | bytes 393224 | tf_op jit(solution)/shard_map/ppermute | solution.py:19
  51.5 7.7 %collective-permute-start.6 = (bf16[256,256]{1,0:T(8,128)(2,1)S(1)}, bf16[256,256]{1,0:T(8,128)(2,1)S(1)}, u32[]{:S(2)}, u32[]{:S(2)}) collective-permute-start(bf16[256,256]{1,0:T(8,128)(2,1)S(1)} %collective-permute-done.5), channel_id=1, source_target_pairs={{0,1},{1,2},{2,3},{3,4},{4,5},{5,6},{6,7},{7,8},{8,9},{9,10},{10,1... | collective-permute-start | bytes 393224 | tf_op jit(solution)/shard_map/ppermute | solution.py:19
  59.2 8.5 %collective-permute-start.7 = (bf16[256,256]{1,0:T(8,128)(2,1)S(1)}, bf16[256,256]{1,0:T(8,128)(2,1)S(1)}, u32[]{:S(2)}, u32[]{:S(2)}) collective-permute-start(bf16[256,256]{1,0:T(8,128)(2,1)S(1)} %collective-permute-done.6), channel_id=1, source_target_pairs={{0,1},{1,2},{2,3},{3,4},{4,5},{5,6},{6,7},{7,8},{8,9},{9,10},{10,1... | collective-permute-start | bytes 393224 | tf_op jit(solution)/shard_map/ppermute | solution.py:19
  67.7 7.6 %collective-permute-start.8 = (bf16[256,256]{1,0:T(8,128)(2,1)S(1)}, bf16[256,256]{1,0:T(8,128)(2,1)S(1)}, u32[]{:S(2)}, u32[]{:S(2)}) collective-permute-start(bf16[256,256]{1,0:T(8,128)(2,1)S(1)} %collective-permute-done.7), channel_id=1, source_target_pairs={{0,1},{1,2},{2,3},{3,4},{4,5},{5,6},{6,7},{7,8},{8,9},{9,10},{10,1... | collective-permute-start | bytes 393224 | tf_op jit(solution)/shard_map/ppermute | solution.py:19
  67.7 259.8 %reduce-scatter.2.cloned.1.call-start = ((), (), s32[]{:S(2)}) async-start(), calls=%async_computation.1 | async-start | bytes 2228224 | tf_op jit(solution)/shard_map/reduce_scatter | solution.py:220
  75.3 7.1 %collective-permute-start.9 = (bf16[256,256]{1,0:T(8,128)(2,1)S(1)}, bf16[256,256]{1,0:T(8,128)(2,1)S(1)}, u32[]{:S(2)}, u32[]{:S(2)}) collective-permute-start(bf16[256,256]{1,0:T(8,128)(2,1)S(1)} %collective-permute-done.8), channel_id=1, source_target_pairs={{0,1},{1,2},{2,3},{3,4},{4,5},{5,6},{6,7},{7,8},{8,9},{9,10},{10,1... | collective-permute-start | bytes 393224 | tf_op jit(solution)/shard_map/ppermute | solution.py:19
  82.5 7.1 %collective-permute-start.10 = (bf16[256,256]{1,0:T(8,128)(2,1)S(1)}, bf16[256,256]{1,0:T(8,128)(2,1)S(1)}, u32[]{:S(2)}, u32[]{:S(2)}) collective-permute-start(bf16[256,256]{1,0:T(8,128)(2,1)S(1)} %collective-permute-done.9), channel_id=1, source_target_pairs={{0,1},{1,2},{2,3},{3,4},{4,5},{5,6},{6,7},{7,8},{8,9},{9,10},{10,1... | collective-permute-start | bytes 393224 | tf_op jit(solution)/shard_map/ppermute | solution.py:19
  89.6 9.6 %collective-permute-start.11 = (bf16[256,256]{1,0:T(8,128)(2,1)S(1)}, bf16[256,256]{1,0:T(8,128)(2,1)S(1)}, u32[]{:S(2)}, u32[]{:S(2)}) collective-permute-start(bf16[256,256]{1,0:T(8,128)(2,1)S(1)} %collective-permute-done.10), channel_id=1, source_target_pairs={{0,1},{1,2},{2,3},{3,4},{4,5},{5,6},{6,7},{7,8},{8,9},{9,10},{10,1... | collective-permute-start | bytes 393224 | tf_op jit(solution)/shard_map/ppermute | solution.py:19
  99.2 8.1 %collective-permute-start.12 = (bf16[256,256]{1,0:T(8,128)(2,1)S(1)}, bf16[256,256]{1,0:T(8,128)(2,1)S(1)}, u32[]{:S(2)}, u32[]{:S(2)}) collective-permute-start(bf16[256,256]{1,0:T(8,128)(2,1)S(1)} %collective-permute-done.11), channel_id=1, source_target_pairs={{0,1},{1,2},{2,3},{3,4},{4,5},{5,6},{6,7},{7,8},{8,9},{9,10},{10,1... | collective-permute-start | bytes 393224 | tf_op jit(solution)/shard_map/ppermute | solution.py:19
  107.3 7.1 %collective-permute-start.13 = (bf16[256,256]{1,0:T(8,128)(2,1)S(1)}, bf16[256,256]{1,0:T(8,128)(2,1)S(1)}, u32[]{:S(2)}, u32[]{:S(2)}) collective-permute-start(bf16[256,256]{1,0:T(8,128)(2,1)S(1)} %collective-permute-done.12), channel_id=1, source_target_pairs={{0,1},{1,2},{2,3},{3,4},{4,5},{5,6},{6,7},{7,8},{8,9},{9,10},{10,1... | collective-permute-start | bytes 393224 | tf_op jit(solution)/shard_map/ppermute | solution.py:19
  114.4 10.7 %collective-permute-start.14 = (bf16[256,256]{1,0:T(8,128)(2,1)S(1)}, bf16[256,256]{1,0:T(8,128)(2,1)S(1)}, u32[]{:S(2)}, u32[]{:S(2)}) collective-permute-start(bf16[256,256]{1,0:T(8,128)(2,1)S(1)} %collective-permute-done.13), channel_id=1, source_target_pairs={{0,1},{1,2},{2,3},{3,4},{4,5},{5,6},{6,7},{7,8},{8,9},{9,10},{10,1... | collective-permute-start | bytes 393224 | tf_op jit(solution)/shard_map/ppermute | solution.py:19
  181.0 12.7 %copy-start = (f32[1024,128]{1,0:T(8,128)S(1)}, f32[1024,128]{1,0:T(8,128)}, u32[]{:S(2)}) copy-start(f32[1024,128]{1,0:T(8,128)} %get-tuple-element.124) | copy-start | bytes 1572868
  188.1 5.4 %collective-permute-start.15 = (bf16[128,512]{1,0:T(8,128)(2,1)S(1)}, bf16[128,512]{1,0:T(8,128)(2,1)S(1)}, u32[]{:S(2)}, u32[]{:S(2)}) collective-permute-start(bf16[128,512]{1,0:T(8,128)(2,1)S(1)} %get-tuple-element.270), channel_id=1, source_target_pairs={{0,8},{1,9},{2,10},{3,11},{4,12},{5,13},{6,14},{7,15},{8,0},{9,1},... | collective-permute-start | bytes 393224 | tf_op jit(solution)/shard_map/ppermute | solution.py:35
  234.9 185.9 %all-gather.7.cloned.1.call-start = ((), (), s32[]{:S(2)}) async-start(), calls=%async_computation.3 | async-start | bytes 13369344 | tf_op jit(solution)/shard_map/all_gather | solution.py:235
  238.8 5.6 %collective-permute-start.16 = (bf16[128,512]{1,0:T(8,128)(2,1)S(1)}, bf16[128,512]{1,0:T(8,128)(2,1)S(1)}, u32[]{:S(2)}, u32[]{:S(2)}) collective-permute-start(bf16[128,512]{1,0:T(8,128)(2,1)S(1)} %slice.59), channel_id=1, source_target_pairs={{0,8},{1,9},{2,10},{3,11},{4,12},{5,13},{6,14},{7,15},{8,0},{9,1},... | collective-permute-start | bytes 393224 | tf_op jit(solution)/shard_map/ppermute | solution.py:35
  435.6 50.1 %collective-permute-start.17 = (bf16[256,8192]{1,0:T(8,128)(2,1)}, bf16[256,8192]{1,0:T(8,128)(2,1)S(1)}, u32[]{:S(2)}, u32[]{:S(2)}) collective-permute-start(bf16[256,8192]{1,0:T(8,128)(2,1)} %fusion.37), channel_id=1, source_target_pairs={{16,0},{32,16},{48,32},{64,48},{80,64},{96,80},{112,96},{17,1},{33... | collective-permute-start | bytes 12582920 | tf_op jit(solution)/shard_map/ppermute | solution.py:41
Sparse Core Ops, SparseCore 0:
  67.9 88.5 all-gather.4
  235.0 92.5 reduce-scatter.1
  329.9 90.8 all-gather.6
